TPU v7x, 256 devices: a whole 4x4x8 slice. The times are simulated.
256 devices in a mesh: win: 32 (over y, z), grp: 8 (over x, core).
Axes of the slice: x: 4, y: 4, z: 8, core: 2. Of those that a mesh axis runs over, the one named last changes fastest.
Arguments:
- points: bfloat16 [32, 8, 512, 512], P('win', 'grp'), may hold values from -6 to 6
- rank: int32 [32, 8, 512], P('win', 'grp'), may hold values from 0 to 16383, as said below
- counts: int32 [8, 32, 8], replicated, may hold values from 1 to 128, 512 in all within a row
- w_qkv_one: bfloat16 [512, 1536], replicated
- w_out_one: bfloat16 [512, 512], replicated, may hold values from -0.25 to 0.25
- w_up: bfloat16 [512, 2048], replicated, may hold values from -0.25 to 0.25
- w_down: bfloat16 [2048, 512], replicated, may hold values from -0.125 to 0.125
- w_qkv_two: bfloat16 [512, 1536], replicated
- w_out_two: bfloat16 [512, 512], replicated, may hold values from -0.25 to 0.25
Outputs:
- encoded: bfloat16 [32, 8, 512, 512], P('win', 'grp')
Inputs may be any that keep to these rules, and one draw needn't show every extreme that they name: Within each of the 8 grp columns, rank over all 32 devices of win is a permutation of 0 to 16383. Each device holds at most 32 points whose rank // 512 is any one owner, and exactly 32 for some owner; each owner receives exactly 32 from some device. For each grp column and owner the 8 counts sum to 512, and the largest is 128.
All inputs are finite; a program needn't handle non-finite values.
Results may differ from a plain program's by a relative error of at most 0.03.
The roundings to bfloat16 on the way count: a program that leaves them out, or rounds other values in their place, can miss the bound.
Values may be sent and summed in bfloat16 or wider, within the bound.
No kernel may reach another device: no remote copies, remote signals or barrier semaphores. Data moves between devices by JAX's collectives and lax.ppermute only.
A program may use at most 128 MiB of HBM per device.

v0:
```python
import jax
import jax.numpy as jnp
from jax import lax
from jax.sharding import PartitionSpec as P

HEAD_DIM = 32
WINDOW_SLOTS = 128
EPSILON = 1e-05
MASKED = -1e30


def normalize(row_data):
    values = row_data.astype(jnp.float32)
    center = values - jnp.mean(values, axis=-1, keepdims=True)
    spread = jnp.mean(center * center, axis=-1, keepdims=True)
    return (center * lax.rsqrt(spread + EPSILON)).astype(jnp.bfloat16)


def project(row_data, weight):
    return jnp.dot(normalize(row_data), weight, preferred_element_type=jnp.float32).astype(
        jnp.bfloat16
    )


def attention_core(packed, valid):
    block_count, width_len, triple = packed.shape
    model_dim = triple // 3
    heads_count = model_dim // HEAD_DIM
    split_heads = packed.reshape(block_count, width_len, 3, heads_count, HEAD_DIM)
    scores = jnp.einsum(
        "bqhe,bkhe->bhqk",
        split_heads[:, :, 0],
        split_heads[:, :, 1],
        preferred_element_type=jnp.float32,
    ) * HEAD_DIM ** (-0.5)
    scores = jnp.where(valid[:, None, None, :], scores, MASKED)
    row_max = jnp.max(scores, axis=-1, keepdims=True)
    weights = jnp.exp(scores - row_max)
    weights = (weights / jnp.sum(weights, axis=-1, keepdims=True)).astype(jnp.bfloat16)
    context = jnp.einsum(
        "bhqk,bkhe->bqhe", weights, split_heads[:, :, 2], preferred_element_type=jnp.float32
    )
    return context.astype(jnp.bfloat16).reshape(block_count * width_len, model_dim)


def residual_add(row_data, context, weight):
    return (
        row_data.astype(jnp.float32) + jnp.dot(context, weight, preferred_element_type=jnp.float32)
    ).astype(jnp.bfloat16)


def feed_forward(row_data, w_up, w_down):
    hidden = jax.nn.gelu(
        jnp.dot(normalize(row_data), w_up, preferred_element_type=jnp.float32), approximate=True
    ).astype(jnp.bfloat16)
    return (
        row_data.astype(jnp.float32) + jnp.dot(hidden, w_down, preferred_element_type=jnp.float32)
    ).astype(jnp.bfloat16)


def on_device(points, rank, counts, w_qkv_one, w_out_one, w_up, w_down, w_qkv_two, w_out_two):
    owner_count = lax.axis_size("win")
    group_count = lax.axis_size("grp")
    win_index = lax.axis_index("win")
    grp_index = lax.axis_index("grp")
    local_points = points.shape[2]
    model_dim = points.shape[3]
    blocks = counts.shape[2]
    slots_all = blocks * WINDOW_SLOTS
    capacity = 2 * local_points // owner_count
    dilation_stride = WINDOW_SLOTS // group_count
    rows_x = points.reshape(local_points, model_dim)
    point_rank = rank.reshape(local_points)
    block_ids = jnp.arange(blocks, dtype=jnp.int32)
    column_counts = lax.dynamic_index_in_dim(counts, grp_index, 0, keepdims=False)
    window_ends = jnp.cumsum(column_counts, axis=1)
    starts = window_ends - column_counts
    owner_dev = point_rank // local_points
    offset = point_rank % local_points
    choose = (owner_dev[:, None] == jnp.arange(owner_count, dtype=jnp.int32)[None, :]).astype(
        jnp.int32
    )
    owner_ends = jnp.sum(choose[:, :, None] * window_ends[None], axis=1)
    owner_starts = jnp.sum(choose[:, :, None] * starts[None], axis=1)
    window = jnp.sum((owner_ends <= offset[:, None]).astype(jnp.int32), axis=1)
    block_pick = (window[:, None] == block_ids[None, :]).astype(jnp.int32)
    dest_slot = window * WINDOW_SLOTS + offset - jnp.sum(block_pick * owner_starts, axis=1)
    peer_order = jnp.sum(choose * (jnp.cumsum(choose, axis=0) - 1), axis=1)
    send_place = owner_dev * capacity + peer_order
    outgoing = (
        jnp.zeros((owner_count * capacity, model_dim), jnp.bfloat16).at[send_place].set(rows_x)
    )
    outgoing_slot = (
        jnp.full((owner_count * capacity,), slots_all, jnp.int32).at[send_place].set(dest_slot)
    )
    arrived, arrived_slot = (
        lax.all_to_all(outgoing, "win", split_axis=0, concat_axis=0, tiled=True),
        lax.all_to_all(outgoing_slot, "win", split_axis=0, concat_axis=0, tiled=True),
    )
    own_counts = lax.dynamic_index_in_dim(column_counts, win_index, 0, keepdims=False)
    column = jnp.arange(WINDOW_SLOTS, dtype=jnp.int32)
    usable_mask = column[None, :] < own_counts[:, None]
    padded_x = (
        jnp.zeros((slots_all, model_dim), jnp.bfloat16).at[arrived_slot].set(arrived, mode="drop")
    )
    packed = project(padded_x, w_qkv_one).reshape(blocks, WINDOW_SLOTS, 3 * model_dim)
    context = attention_core(packed, usable_mask)
    first_pad = feed_forward(residual_add(padded_x, context, w_out_one), w_up, w_down)
    mask_send = usable_mask.astype(jnp.bfloat16).reshape(blocks, dilation_stride, group_count)
    dilated_rows = lax.all_to_all(
        first_pad.reshape(blocks, dilation_stride, group_count, model_dim),
        "grp",
        split_axis=2,
        concat_axis=1,
        tiled=True,
    )
    valid_marks = lax.all_to_all(mask_send, "grp", split_axis=2, concat_axis=1, tiled=True)
    block_count = dilated_rows.shape[0]
    flat_rows = dilated_rows.reshape(block_count * WINDOW_SLOTS, model_dim)
    packed_two = project(flat_rows, w_qkv_two).reshape(block_count, WINDOW_SLOTS, 3 * model_dim)
    head_context = attention_core(packed_two, valid_marks.reshape(block_count, WINDOW_SLOTS) > 0.5)
    mixed_rows = residual_add(flat_rows, head_context, w_out_two).reshape(
        block_count, WINDOW_SLOTS, 1, model_dim
    )
    second_pad = lax.all_to_all(mixed_rows, "grp", split_axis=1, concat_axis=2, tiled=True).reshape(
        slots_all, model_dim
    )
    returning = jnp.take(second_pad, arrived_slot, axis=0, mode="fill", fill_value=0)
    returned = lax.all_to_all(returning, "win", split_axis=0, concat_axis=0, tiled=True)
    encoded = jnp.take(returned, send_place, axis=0)
    return encoded.reshape(1, 1, local_points, model_dim)


def solution(mesh):
    return jax.shard_map(
        on_device,
        mesh=mesh,
        in_specs=(
            P("win", "grp", None, None),
            P("win", "grp", None),
            P(),
            P(),
            P(),
            P(),
            P(),
            P(),
            P(),
        ),
        out_specs=P("win", "grp", None, None),
        check_vma=False,
    )
```

profile of v0, /device:TPU:32, one launch (start us, length us, event | category | flops | bytes accessed | tf_op | source)
XLA Modules:
  0.0 210.3 jit_solution(3294899480315234753)
XLA Ops:
  0.0 0.8 dynamic-slice_bitcast_fusion
  1.6 0.7 add_select_fusion.1
  2.3 0.7 add_select_fusion
  3.1 1.2 reduce-window.6
  4.6 0.7 compare_select_fusion.2
  5.5 0.7 add_subtract_fusion
  6.2 2.4 %scatter_custom_fusion = s32[1024]{0:T(1024)S(1)} fusion(s32[512]{0:T(512)S(1)} %bitcast.161, s32[512]{0:T(512)S(1)} %add_subtract_fusion, s32[]{:T(128)} %constant.120.clone.1), kind=kCustom, calls=%fused_computation.140 | custom fusion | bytes 4100 | tf_op jit(solution)/shard_map/scatter | solution.py:94
  8.7 0.7 all_to_all.49
  9.4 11.4 %all-to-all-start = ((s32[32,32,1]{1,2,0:T(1,128)}), s32[32,32,1]{1,2,0:T(1,128)S(1)}, u32[]{:S(2)}, u32[]{:S(2)}) async-start(s32[32,32,1]{1,2,0:T(1,128)} %all_to_all.49), calls=%async_computation | async-start | bytes 32768 | tf_op jit(solution)/shard_map/all_to_all | solution.py:98
  20.7 4.0 %scatter_custom_fusion.1 = bf16[1024,512]{1,0:T(8,128)(2,1)} fusion(s32[512]{0:T(512)S(1)} %bitcast.162, bf16[1,1,512,512]{3,2,1,0:T(8,128)(2,1)} %param.9, bf16[]{:T(256)} %constant.126.clone.1), kind=kCustom, calls=%fused_computation.82 | custom fusion | bytes 1572866 | tf_op jit(solution)/shard_map/scatter | solution.py:91
  24.7 4.6 %all-to-all-done = s32[32,32,1]{1,2,0:T(1,128)S(1)} async-done(((s32[32,32,1]{1,2,0:T(1,128)}), s32[32,32,1]{1,2,0:T(1,128)S(1)}, u32[]{:S(2)}, u32[]{:S(2)}) %all-to-all-start) | async-done | bytes 4128 | tf_op jit(solution)/shard_map/all_to_all | solution.py:98
  29.3 5.2 %all-to-all-start.1 = ((bf16[32,32,512]{2,1,0:T(8,128)(2,1)}), bf16[32,32,512]{2,1,0:T(8,128)(2,1)S(1)}, u32[]{:S(2)}, u32[]{:S(2)}) async-start(bf16[32,32,512]{2,1,0:T(8,128)(2,1)} %bitcast.12), calls=%async_computation.1 | async-start | bytes 2097152 | tf_op jit(solution)/shard_map/all_to_all | solution.py:97
  34.5 0.9 dynamic-slice_reduce_fusion
  36.7 0.7 reduce.9
  37.6 24.9 %all-to-all-done.1 = bf16[32,32,512]{2,1,0:T(8,128)(2,1)S(1)} async-done(((bf16[32,32,512]{2,1,0:T(8,128)(2,1)}), bf16[32,32,512]{2,1,0:T(8,128)(2,1)S(1)}, u32[]{:S(2)}, u32[]{:S(2)}) %all-to-all-start.1) | async-done | bytes 1048608 | tf_op jit(solution)/shard_map/all_to_all | solution.py:97
  62.5 4.3 %all-to-all-start.3 = ((bf16[8,16,8]{1,0,2:T(8,128)(2,1)}), bf16[8,16,8]{1,0,2:T(8,128)(2,1)S(1)}, u32[]{:S(2)}, u32[]{:S(2)}) async-start(bf16[8,16,8]{1,0,2:T(8,128)(2,1)} %compare_convert_fusion), calls=%async_computation.3 | async-start | bytes 32768 | tf_op jit(solution)/shard_map/all_to_all | solution.py:117
  66.8 5.8 %scatter_custom_fusion.2 = bf16[1024,512]{1,0:T(8,128)(2,1)S(1)} fusion(s32[1024]{0:T(1024)S(1)} %bitcast.159, bf16[1024,512]{1,0:T(8,128)(2,1)} %bitcast.151, bf16[]{:T(256)} %constant.126.clone.1), kind=kCustom, calls=%fused_computation.84 | custom fusion | bytes 1049088 | tf_op jit(solution)/shard_map/scatter | solution.py:104
  73.4 4.9 %convolution_convert_fusion.1 = bf16[1024,1536]{1,0:T(8,128)(2,1)} fusion(bf16[512,1536]{1,0:T(8,128)(2,1)} %param.12, bf16[1024,512]{1,0:T(8,128)(2,1)S(1)} %scatter_custom_fusion.2, f32[1024]{0:T(1024)S(1)} %add_rsqrt_fusion.1, f32[1024]{0:T(1024)S(1)} %broadcast_multiply_fusion.1), kind=kOutput, calls=%fused_computation.34 | convolution fusion | flops 1614282752 | bytes 5775360 | tf_op jit(solution)/shard_map/dot_general | solution.py:20
  78.3 4.7 %copy.120 = bf16[1024,1536]{0,1:T(8,128)(2,1)} copy(bf16[1024,1536]{1,0:T(8,128)(2,1)} %convolution_convert_fusion.1) | data formatting | bytes 6291456 | tf_op jit(solution)/shard_map/convert_element_type | solution.py:20
  83.0 2.7 %copy.155 = bf16[192,8,8,128]{3,2,1,0:T(8,128)(2,1)S(1)} copy(bf16[192,8,8,128]{3,1,2,0:T(8,128)(2,1)} %bitcast.145) | data formatting | bytes 6291456
  86.1 1.3 fusion.52
  87.4 3.5 %fusion.86 = (f32[8,16,128]{2,1,0:T(8,128)S(1)}, f32[8,16,128,128]{2,3,1,0:T(8,128)S(1)}) fusion(f32[8,16,128,128]{2,3,1,0:T(8,128)S(1)} %fusion.52, pred[8,128]{1,0:T(8,128)(4,1)S(1)} %iota_compare_fusion.3), kind=kOutput, calls=%fused_computation.158 | output fusion | flops 12583039 | bytes 16843776 | tf_op jit(solution)/shard_map/sub | solution.py:38
  90.9 1.2 fusion.41
  92.1 0.7 copy.125
  92.8 0.8 convert_reduce_fusion
  93.6 1.0 copy-done.3
  95.1 7.0 %fusion.31 = bf16[1024,512]{1,0:T(8,128)(2,1)S(1)} fusion(bf16[1024,512]{1,0:T(8,128)(2,1)} %copy-done.3, bf16[2048,512]{1,0:T(8,128)(2,1)S(1)} %copy-done, bf16[512,2048]{1,0:T(8,128)(2,1)} %param.14, f32[1024]{0:T(1024)S(1)} %add_rsqrt_fusion, f32[1024]{0:T(1024)S(1)} %broadcast_multiply_fusion), kind=kOutput, calls=%fused_computation.50 | convolution fusion | flops 4317511680 | bytes 6299648 | tf_op jit(solution)/shard_map/dot_general | solution.py:57
  102.2 1.3 copy.126
  103.5 4.8 %all-to-all-start.2 = ((bf16[8,16,8,512]{3,1,0,2:T(8,128)(2,1)}), bf16[8,16,8,512]{3,1,0,2:T(8,128)(2,1)S(1)}, u32[]{:S(2)}, u32[]{:S(2)}) async-start(bf16[8,16,8,512]{3,1,0,2:T(8,128)(2,1)} %copy.126), calls=%async_computation.2 | async-start | bytes 2097152 | tf_op jit(solution)/shard_map/all_to_all | solution.py:110
  108.4 15.8 %all-to-all-done.2 = bf16[8,16,8,512]{3,1,0,2:T(8,128)(2,1)S(1)} async-done(((bf16[8,16,8,512]{3,1,0,2:T(8,128)(2,1)}), bf16[8,16,8,512]{3,1,0,2:T(8,128)(2,1)S(1)}, u32[]{:S(2)}, u32[]{:S(2)}) %all-to-all-start.2) | async-done | bytes 1048608 | tf_op jit(solution)/shard_map/all_to_all | solution.py:110
  126.1 0.8 copy-done.5
  126.9 3.5 %convolution_convert_fusion = bf16[1024,1536]{1,0:T(8,128)(2,1)} fusion(bf16[1024,512]{1,0:T(8,128)(2,1)S(1)} %fusion.33, bf16[512,1536]{1,0:T(8,128)(2,1)S(1)} %copy-done.5), kind=kOutput, calls=%fused_computation.33 | convolution fusion | flops 1612185600 | bytes 5767168 | tf_op jit(solution)/shard_map/dot_general | solution.py:20
  130.3 4.7 %copy.133 = bf16[1024,1536]{0,1:T(8,128)(2,1)} copy(bf16[1024,1536]{1,0:T(8,128)(2,1)} %convolution_convert_fusion) | data formatting | bytes 6291456 | tf_op jit(solution)/shard_map/convert_element_type | solution.py:20
  135.0 2.7 %copy.157 = bf16[192,8,8,128]{3,2,1,0:T(8,128)(2,1)S(1)} copy(bf16[192,8,8,128]{3,1,2,0:T(8,128)(2,1)} %bitcast.146) | data formatting | bytes 6291456
  138.1 1.3 fusion.51
  139.4 3.5 %fusion.87 = (f32[8,16,128]{2,1,0:T(8,128)S(1)}, f32[8,16,128,128]{2,3,1,0:T(8,128)S(1)}) fusion(f32[8,16,128,128]{2,3,1,0:T(8,128)S(1)} %fusion.51, pred[8,128]{1,0:T(8,128)(4,1)S(1)} %gt.23), kind=kOutput, calls=%fused_computation.159 | output fusion | flops 12583039 | bytes 16843776 | tf_op jit(solution)/shard_map/sub | solution.py:38
  142.9 1.2 fusion.42
  144.1 0.7 copy.139
  144.8 0.7 fusion.34
  145.5 1.6 copy.140
  147.1 3.6 %all-to-all-start.4 = ((bf16[8,128,1,512]{3,0,2,1:T(8,128)(2,1)}), bf16[8,128,1,512]{3,0,2,1:T(8,128)(2,1)S(1)}, u32[]{:S(2)}, u32[]{:S(2)}) async-start(bf16[8,128,1,512]{3,0,2,1:T(8,128)(2,1)} %copy.140), calls=%async_computation.4 | async-start | bytes 2097152 | tf_op jit(solution)/shard_map/all_to_all | solution.py:125
  150.7 15.8 %all-to-all-done.4 = bf16[8,128,1,512]{3,0,2,1:T(8,128)(2,1)S(1)} async-done(((bf16[8,128,1,512]{3,0,2,1:T(8,128)(2,1)}), bf16[8,128,1,512]{3,0,2,1:T(8,128)(2,1)S(1)}, u32[]{:S(2)}, u32[]{:S(2)}) %all-to-all-start.4) | async-done | bytes 1048608 | tf_op jit(solution)/shard_map/all_to_all | solution.py:125
  167.1 4.0 %gather_fusion = bf16[1024,512]{1,0:T(8,128)(2,1)S(1)} fusion(bf16[1024,512]{1,0:T(8,128)(2,1)S(1)} %bitcast.141, s32[1024]{0:T(1024)S(1)} %broadcast_clamp_fusion), kind=kCustom, calls=%fused_computation | custom fusion | bytes 2101248 | tf_op jit(solution)/shard_map/jit(_take)/gather | solution.py:128
  171.1 1.2 broadcast_select_fusion
  172.3 5.2 %all-to-all-start.5 = ((bf16[32,32,512]{2,1,0:T(8,128)(2,1)}), bf16[32,32,512]{2,1,0:T(8,128)(2,1)S(1)}, u32[]{:S(2)}, u32[]{:S(2)}) async-start(bf16[32,32,512]{2,1,0:T(8,128)(2,1)} %broadcast_select_fusion), calls=%async_computation.5 | async-start | bytes 2097152 | tf_op jit(solution)/shard_map/all_to_all | solution.py:129
  177.5 28.2 %all-to-all-done.5 = bf16[32,32,512]{2,1,0:T(8,128)(2,1)S(1)} async-done(((bf16[32,32,512]{2,1,0:T(8,128)(2,1)}), bf16[32,32,512]{2,1,0:T(8,128)(2,1)S(1)}, u32[]{:S(2)}, u32[]{:S(2)}) %all-to-all-start.5) | async-done | bytes 1048608 | tf_op jit(solution)/shard_map/all_to_all | solution.py:129
  205.7 2.6 %gather_fusion.1 = bf16[512,512]{1,0:T(8,128)(2,1)} fusion(bf16[1024,512]{1,0:T(8,128)(2,1)S(1)} %bitcast.142, s32[1024]{0:T(1024)S(1)} %pad_clamp_fusion), kind=kCustom, calls=%fused_computation.1 | custom fusion | bytes 1050624 | tf_op jit(solution)/shard_map/jit(_take)/gather | solution.py:130
  208.3 2.0 bitcast_select_fusion
  (59 shorter events, 7.4 us)
Async XLA Ops:
  0.0 95.1 %copy-start = (bf16[2048,512]{1,0:T(8,128)(2,1)S(1)}, bf16[2048,512]{1,0:T(8,128)(2,1)}, u32[]{:S(2)}) copy-start(bf16[2048,512]{1,0:T(8,128)(2,1)} %param.15) | copy-start | bytes 6291460
  9.4 19.9 %all-to-all-start = ((s32[32,32,1]{1,2,0:T(1,128)}), s32[32,32,1]{1,2,0:T(1,128)S(1)}, u32[]{:S(2)}, u32[]{:S(2)}) async-start(s32[32,32,1]{1,2,0:T(1,128)} %all_to_all.49), calls=%async_computation | async-start | bytes 32768 | tf_op jit(solution)/shard_map/all_to_all | solution.py:98
  29.3 33.2 %all-to-all-start.1 = ((bf16[32,32,512]{2,1,0:T(8,128)(2,1)}), bf16[32,32,512]{2,1,0:T(8,128)(2,1)S(1)}, u32[]{:S(2)}, u32[]{:S(2)}) async-start(bf16[32,32,512]{2,1,0:T(8,128)(2,1)} %bitcast.12), calls=%async_computation.1 | async-start | bytes 2097152 | tf_op jit(solution)/shard_map/all_to_all | solution.py:97
  62.5 4.3 %copy-start.2 = (bf16[32,32,512]{2,1,0:T(8,128)(2,1)}, bf16[32,32,512]{2,1,0:T(8,128)(2,1)S(1)}, u32[]{:S(2)}) copy-start(bf16[32,32,512]{2,1,0:T(8,128)(2,1)S(1)} %all-to-all-done.1) | copy-start | bytes 3145732
  62.5 41.0 %all-to-all-start.3 = ((bf16[8,16,8]{1,0,2:T(8,128)(2,1)}), bf16[8,16,8]{1,0,2:T(8,128)(2,1)S(1)}, u32[]{:S(2)}, u32[]{:S(2)}) async-start(bf16[8,16,8]{1,0,2:T(8,128)(2,1)} %compare_convert_fusion), calls=%async_computation.3 | async-start | bytes 32768 | tf_op jit(solution)/shard_map/all_to_all | solution.py:117
  90.8 1.9 copy-start.6
  93.6 1.0 copy-start.3
  103.5 20.7 %all-to-all-start.2 = ((bf16[8,16,8,512]{3,1,0,2:T(8,128)(2,1)}), bf16[8,16,8,512]{3,1,0,2:T(8,128)(2,1)S(1)}, u32[]{:S(2)}, u32[]{:S(2)}) async-start(bf16[8,16,8,512]{3,1,0,2:T(8,128)(2,1)} %copy.126), calls=%async_computation.2 | async-start | bytes 2097152 | tf_op jit(solution)/shard_map/all_to_all | solution.py:110
  125.5 1.4 copy-start.5
  142.9 1.9 copy-start.4
  147.1 19.4 %all-to-all-start.4 = ((bf16[8,128,1,512]{3,0,2,1:T(8,128)(2,1)}), bf16[8,128,1,512]{3,0,2,1:T(8,128)(2,1)S(1)}, u32[]{:S(2)}, u32[]{:S(2)}) async-start(bf16[8,128,1,512]{3,0,2,1:T(8,128)(2,1)} %copy.140), calls=%async_computation.4 | async-start | bytes 2097152 | tf_op jit(solution)/shard_map/all_to_all | solution.py:125
  172.3 33.4 %all-to-all-start.5 = ((bf16[32,32,512]{2,1,0:T(8,128)(2,1)}), bf16[32,32,512]{2,1,0:T(8,128)(2,1)S(1)}, u32[]{:S(2)}, u32[]{:S(2)}) async-start(bf16[32,32,512]{2,1,0:T(8,128)(2,1)} %broadcast_select_fusion), calls=%async_computation.5 | async-start | bytes 2097152 | tf_op jit(solution)/shard_map/all_to_all | solution.py:129
  177.5 32.8 %copy-start.1 = (bf16[2048,512]{1,0:T(8,128)(2,1)S(1)}, bf16[2048,512]{1,0:T(8,128)(2,1)}, u32[]{:S(2)}) copy-start(bf16[2048,512]{1,0:T(8,128)(2,1)} %param.15) | copy-start | bytes 6291460
where the time goes:
time: 211 us; the launch traced here: 210 us
  waiting for transfers between devices  89.3 us (42%)
  local copies, waits for them, and re-layouts  44.9 us (21%)
  starting transfers between devices  34.4 us (16%)
  matrix products  22 us (10%)
  other arithmetic  19.3 us (9%)
    all_to_all x1, waiting for transfers between devices, on_device(): lax.all_to_all(returning, 'win', split_axis=0, concat_axis=0, tiled=True)  28.2 us
    all_to_all x1, waiting for transfers between devices, on_device(): lax.all_to_all(outgoing, 'win', split_axis=0, concat_axis=0, tiled=True)  24.9 us
    all_to_all x1, waiting for transfers between devices, on_device(): lax.all_to_all(mixed_rows, 'grp', split_axis=1, concat_axis=2, tiled=True)  15.8 us
    all_to_all x1, waiting for transfers between devices, on_device(): lax.all_to_all(first_pad.reshape(blocks, dilation_stride, group_count, mo...  15.8 us
    all_to_all x1, starting transfers between devices, on_device(): lax.all_to_all(outgoing_slot, 'win', split_axis=0, concat_axis=0, tiled=T...  11.4 us
    convert_element_type x2, local copies, waits for them, and re-layouts, project(): jnp.dot(normalize(row_data), weight, preferred_element_type=jnp.float32)  9.38 us
    dot_general x2, matrix products, project(): jnp.dot(normalize(row_data), weight, preferred_element_type=jnp.float32)  8.39 us
    unnamed x16, local copies, waits for them, and re-layouts  7.21 us
  transfers between devices with their start and end apart: 6, of which 5 were waited for; matrix products, arithmetic and copies ran while one was open for 20% of the time, Pallas kernels for 0%

commit v1 on v0

--- a/solution.py
+++ b/solution.py
@@ -122,9 +122,10 @@
     mixed_rows = residual_add(flat_rows, head_context, w_out_two).reshape(
         block_count, WINDOW_SLOTS, 1, model_dim
     )
-    second_pad = lax.all_to_all(mixed_rows, "grp", split_axis=1, concat_axis=2, tiled=True).reshape(
-        slots_all, model_dim
-    )
+    second_pad = jnp.concatenate(
+        lax.all_to_all(jnp.stack(jnp.split(mixed_rows, lax.axis_size("grp"), axis=1)), "grp", 0, 0),
+        axis=2,
+    ).reshape(slots_all, model_dim)
     returning = jnp.take(second_pad, arrived_slot, axis=0, mode="fill", fill_value=0)
     returned = lax.all_to_all(returning, "win", split_axis=0, concat_axis=0, tiled=True)
     encoded = jnp.take(returned, send_place, axis=0)

time: 211 us -> 215 us (1.019)
  local copies, waits for them, and re-layouts: 44.9 us -> 48.7 us
    unnamed x16 -> x23, local copies, waits for them, and re-layouts: 7.21 us -> 11.8 us
where the time goes in v1:
time: 215 us; the launch traced here: 214 us
  waiting for transfers between devices  89.3 us (42%)
  local copies, waits for them, and re-layouts  48.7 us (23%)
  starting transfers between devices  34.4 us (16%)
  matrix products  22 us (10%)
  other arithmetic  19.3 us (9%)
    all_to_all x1, waiting for transfers between devices, on_device(): lax.all_to_all(returning, 'win', split_axis=0, concat_axis=0, tiled=True)  28.2 us
    all_to_all x1, waiting for transfers between devices, on_device(): lax.all_to_all(outgoing, 'win', split_axis=0, concat_axis=0, tiled=True)  24.9 us
    all_to_all x1, waiting for transfers between devices, on_device(): lax.all_to_all(jnp.stack(jnp.split(mixed_rows, lax.axis_size('grp'), axis...  15.8 us
    all_to_all x1, waiting for transfers between devices, on_device(): lax.all_to_all(first_pad.reshape(blocks, dilation_stride, group_count, mo...  15.8 us
    unnamed x23, local copies, waits for them, and re-layouts  11.8 us
    all_to_all x1, starting transfers between devices, on_device(): lax.all_to_all(outgoing_slot, 'win', split_axis=0, concat_axis=0, tiled=T...  11.4 us
    convert_element_type x2, local copies, waits for them, and re-layouts, project(): jnp.dot(normalize(row_data), weight, preferred_element_type=jnp.float32)  9.38 us
    dot_general x2, matrix products, project(): jnp.dot(normalize(row_data), weight, preferred_element_type=jnp.float32)  8.39 us
  transfers between devices with their start and end apart: 6, of which 5 were waited for; matrix products, arithmetic and copies ran while one was open for 20% of the time, Pallas kernels for 0%

profile of v1, /device:TPU:32, one launch (start us, length us, event | category | flops | bytes accessed | tf_op | source)
XLA Modules:
  0.0 214.1 jit_solution(17143753783236605721)
XLA Ops:
  0.0 0.8 dynamic-slice_bitcast_fusion
  0.9 0.7 fusion.78
  1.6 0.7 add_select_fusion.1
  2.3 0.7 add_select_fusion
  3.1 1.2 reduce-window.6
  4.6 0.7 compare_select_fusion.2
  5.5 0.7 add_subtract_fusion
  6.2 2.4 %scatter_custom_fusion = s32[1024]{0:T(1024)S(1)} fusion(s32[512]{0:T(512)S(1)} %bitcast.198, s32[512]{0:T(512)S(1)} %add_subtract_fusion, s32[]{:T(128)} %constant.120.clone.1), kind=kCustom, calls=%fused_computation.156 | custom fusion | bytes 4100 | tf_op jit(solution)/shard_map/scatter | solution.py:94
  8.7 0.7 all_to_all.41
  9.4 11.4 %all-to-all-start = ((s32[32,32,1]{1,2,0:T(1,128)}), s32[32,32,1]{1,2,0:T(1,128)S(1)}, u32[]{:S(2)}, u32[]{:S(2)}) async-start(s32[32,32,1]{1,2,0:T(1,128)} %all_to_all.41), calls=%async_computation | async-start | bytes 32768 | tf_op jit(solution)/shard_map/all_to_all | solution.py:98
  20.7 4.0 %scatter_custom_fusion.1 = bf16[1024,512]{1,0:T(8,128)(2,1)} fusion(s32[512]{0:T(512)S(1)} %bitcast.199, bf16[1,1,512,512]{3,2,1,0:T(8,128)(2,1)} %param.9, bf16[]{:T(256)} %constant.126.clone.1), kind=kCustom, calls=%fused_computation.82 | custom fusion | bytes 1572866 | tf_op jit(solution)/shard_map/scatter | solution.py:91
  24.7 4.6 %all-to-all-done = s32[32,32,1]{1,2,0:T(1,128)S(1)} async-done(((s32[32,32,1]{1,2,0:T(1,128)}), s32[32,32,1]{1,2,0:T(1,128)S(1)}, u32[]{:S(2)}, u32[]{:S(2)}) %all-to-all-start) | async-done | bytes 4128 | tf_op jit(solution)/shard_map/all_to_all | solution.py:98
  29.3 5.2 %all-to-all-start.1 = ((bf16[32,32,512]{2,1,0:T(8,128)(2,1)}), bf16[32,32,512]{2,1,0:T(8,128)(2,1)S(1)}, u32[]{:S(2)}, u32[]{:S(2)}) async-start(bf16[32,32,512]{2,1,0:T(8,128)(2,1)} %bitcast.12), calls=%async_computation.1 | async-start | bytes 2097152 | tf_op jit(solution)/shard_map/all_to_all | solution.py:97
  34.5 0.9 dynamic-slice_reduce_fusion
  36.7 0.7 reduce.9
  37.6 24.9 %all-to-all-done.1 = bf16[32,32,512]{2,1,0:T(8,128)(2,1)S(1)} async-done(((bf16[32,32,512]{2,1,0:T(8,128)(2,1)}), bf16[32,32,512]{2,1,0:T(8,128)(2,1)S(1)}, u32[]{:S(2)}, u32[]{:S(2)}) %all-to-all-start.1) | async-done | bytes 1048608 | tf_op jit(solution)/shard_map/all_to_all | solution.py:97
  62.5 4.3 %all-to-all-start.3 = ((bf16[8,16,8]{1,0,2:T(8,128)(2,1)}), bf16[8,16,8]{1,0,2:T(8,128)(2,1)S(1)}, u32[]{:S(2)}, u32[]{:S(2)}) async-start(bf16[8,16,8]{1,0,2:T(8,128)(2,1)} %compare_convert_fusion), calls=%async_computation.3 | async-start | bytes 32768 | tf_op jit(solution)/shard_map/all_to_all | solution.py:117
  66.8 5.8 %scatter_custom_fusion.2 = bf16[1024,512]{1,0:T(8,128)(2,1)S(1)} fusion(s32[1024]{0:T(1024)S(1)} %bitcast.196, bf16[1024,512]{1,0:T(8,128)(2,1)} %bitcast.188, bf16[]{:T(256)} %constant.126.clone.1), kind=kCustom, calls=%fused_computation.84 | custom fusion | bytes 1049088 | tf_op jit(solution)/shard_map/scatter | solution.py:104
  73.4 4.9 %convolution_convert_fusion.1 = bf16[1024,1536]{1,0:T(8,128)(2,1)} fusion(bf16[512,1536]{1,0:T(8,128)(2,1)} %param.12, bf16[1024,512]{1,0:T(8,128)(2,1)S(1)} %scatter_custom_fusion.2, f32[1024]{0:T(1024)S(1)} %add_rsqrt_fusion.1, f32[1024]{0:T(1024)S(1)} %broadcast_multiply_fusion.1), kind=kOutput, calls=%fused_computation.34 | convolution fusion | flops 1614282752 | bytes 5775360 | tf_op jit(solution)/shard_map/dot_general | solution.py:20
  78.3 4.7 %copy.117 = bf16[1024,1536]{0,1:T(8,128)(2,1)} copy(bf16[1024,1536]{1,0:T(8,128)(2,1)} %convolution_convert_fusion.1) | data formatting | bytes 6291456 | tf_op jit(solution)/shard_map/convert_element_type | solution.py:20
  83.0 2.7 %copy.151 = bf16[192,8,8,128]{3,2,1,0:T(8,128)(2,1)S(1)} copy(bf16[192,8,8,128]{3,1,2,0:T(8,128)(2,1)} %bitcast.175) | data formatting | bytes 6291456
  86.1 1.3 fusion.52
  87.4 3.5 %fusion.94 = (f32[8,16,128]{2,1,0:T(8,128)S(1)}, f32[8,16,128,128]{2,3,1,0:T(8,128)S(1)}) fusion(f32[8,16,128,128]{2,3,1,0:T(8,128)S(1)} %fusion.52, pred[8,128]{1,0:T(8,128)(4,1)S(1)} %iota_compare_fusion.3), kind=kOutput, calls=%fused_computation.174 | output fusion | flops 12583039 | bytes 16843776 | tf_op jit(solution)/shard_map/sub | solution.py:38
  90.9 1.2 fusion.41
  92.1 0.7 copy.122
  92.8 0.8 convert_reduce_fusion
  93.6 1.0 copy-done.3
  95.1 7.0 %fusion.31 = bf16[1024,512]{1,0:T(8,128)(2,1)S(1)} fusion(bf16[1024,512]{1,0:T(8,128)(2,1)} %copy-done.3, bf16[2048,512]{1,0:T(8,128)(2,1)S(1)} %copy-done, bf16[512,2048]{1,0:T(8,128)(2,1)} %param.14, f32[1024]{0:T(1024)S(1)} %add_rsqrt_fusion, f32[1024]{0:T(1024)S(1)} %broadcast_multiply_fusion), kind=kOutput, calls=%fused_computation.50 | convolution fusion | flops 4317511680 | bytes 6299648 | tf_op jit(solution)/shard_map/dot_general | solution.py:57
  102.2 1.3 copy.123
  103.5 4.8 %all-to-all-start.2 = ((bf16[8,16,8,512]{3,1,0,2:T(8,128)(2,1)}), bf16[8,16,8,512]{3,1,0,2:T(8,128)(2,1)S(1)}, u32[]{:S(2)}, u32[]{:S(2)}) async-start(bf16[8,16,8,512]{3,1,0,2:T(8,128)(2,1)} %copy.123), calls=%async_computation.2 | async-start | bytes 2097152 | tf_op jit(solution)/shard_map/all_to_all | solution.py:110
  108.4 15.8 %all-to-all-done.2 = bf16[8,16,8,512]{3,1,0,2:T(8,128)(2,1)S(1)} async-done(((bf16[8,16,8,512]{3,1,0,2:T(8,128)(2,1)}), bf16[8,16,8,512]{3,1,0,2:T(8,128)(2,1)S(1)}, u32[]{:S(2)}, u32[]{:S(2)}) %all-to-all-start.2) | async-done | bytes 1048608 | tf_op jit(solution)/shard_map/all_to_all | solution.py:110
  126.1 0.8 copy-done.5
  126.9 3.5 %convolution_convert_fusion = bf16[1024,1536]{1,0:T(8,128)(2,1)} fusion(bf16[1024,512]{1,0:T(8,128)(2,1)S(1)} %fusion.33, bf16[512,1536]{1,0:T(8,128)(2,1)S(1)} %copy-done.5), kind=kOutput, calls=%fused_computation.33 | convolution fusion | flops 1612185600 | bytes 5767168 | tf_op jit(solution)/shard_map/dot_general | solution.py:20
  130.3 4.7 %copy.130 = bf16[1024,1536]{0,1:T(8,128)(2,1)} copy(bf16[1024,1536]{1,0:T(8,128)(2,1)} %convolution_convert_fusion) | data formatting | bytes 6291456 | tf_op jit(solution)/shard_map/convert_element_type | solution.py:20
  135.0 2.7 %copy.153 = bf16[192,8,8,128]{3,2,1,0:T(8,128)(2,1)S(1)} copy(bf16[192,8,8,128]{3,1,2,0:T(8,128)(2,1)} %bitcast.176) | data formatting | bytes 6291456
  138.1 1.3 fusion.51
  139.4 3.5 %fusion.95 = (f32[8,16,128]{2,1,0:T(8,128)S(1)}, f32[8,16,128,128]{2,3,1,0:T(8,128)S(1)}) fusion(f32[8,16,128,128]{2,3,1,0:T(8,128)S(1)} %fusion.51, pred[8,128]{1,0:T(8,128)(4,1)S(1)} %gt.23), kind=kOutput, calls=%fused_computation.175 | output fusion | flops 12583039 | bytes 16843776 | tf_op jit(solution)/shard_map/sub | solution.py:38
  142.9 1.2 fusion.42
  144.1 0.7 copy.136
  144.8 0.7 fusion.34
  150.8 3.6 %all-to-all-start.4 = ((bf16[8,8,16,1,512]{4,2,1,3,0:T(8,128)(2,1)}), bf16[8,8,16,1,512]{4,2,1,3,0:T(8,128)(2,1)S(1)}, u32[]{:S(2)}, u32[]{:S(2)}) async-start(bf16[8,8,16,1,512]{4,2,1,3,0:T(8,128)(2,1)} %fusion.64), calls=%async_computation.4 | async-start | bytes 2097152 | tf_op jit(solution)/shard_map/all_to_all | solution.py:126
  154.4 15.8 %all-to-all-done.4 = bf16[8,8,16,1,512]{4,2,1,3,0:T(8,128)(2,1)S(1)} async-done(((bf16[8,8,16,1,512]{4,2,1,3,0:T(8,128)(2,1)}), bf16[8,8,16,1,512]{4,2,1,3,0:T(8,128)(2,1)S(1)}, u32[]{:S(2)}, u32[]{:S(2)}) %all-to-all-start.4) | async-done | bytes 1048608 | tf_op jit(solution)/shard_map/all_to_all | solution.py:126
  170.8 4.0 %gather_fusion = bf16[1024,512]{1,0:T(8,128)(2,1)S(1)} fusion(bf16[1024,512]{1,0:T(8,128)(2,1)S(1)} %bitcast.171, s32[1024]{0:T(1024)S(1)} %broadcast_clamp_fusion), kind=kCustom, calls=%fused_computation | custom fusion | bytes 2101248 | tf_op jit(solution)/shard_map/jit(_take)/gather | solution.py:129
  174.8 1.2 broadcast_select_fusion
  176.0 5.2 %all-to-all-start.5 = ((bf16[32,32,512]{2,1,0:T(8,128)(2,1)}), bf16[32,32,512]{2,1,0:T(8,128)(2,1)S(1)}, u32[]{:S(2)}, u32[]{:S(2)}) async-start(bf16[32,32,512]{2,1,0:T(8,128)(2,1)} %broadcast_select_fusion), calls=%async_computation.5 | async-start | bytes 2097152 | tf_op jit(solution)/shard_map/all_to_all | solution.py:130
  181.3 28.2 %all-to-all-done.5 = bf16[32,32,512]{2,1,0:T(8,128)(2,1)S(1)} async-done(((bf16[32,32,512]{2,1,0:T(8,128)(2,1)}), bf16[32,32,512]{2,1,0:T(8,128)(2,1)S(1)}, u32[]{:S(2)}, u32[]{:S(2)}) %all-to-all-start.5) | async-done | bytes 1048608 | tf_op jit(solution)/shard_map/all_to_all | solution.py:130
  209.5 2.6 %gather_fusion.1 = bf16[512,512]{1,0:T(8,128)(2,1)} fusion(bf16[1024,512]{1,0:T(8,128)(2,1)S(1)} %bitcast.172, s32[1024]{0:T(1024)S(1)} %pad_clamp_fusion), kind=kCustom, calls=%fused_computation.1 | custom fusion | bytes 1050624 | tf_op jit(solution)/shard_map/jit(_take)/gather | solution.py:131
  212.1 2.0 bitcast_select_fusion
  (66 shorter events, 12.0 us)
Async XLA Ops:
  0.0 95.1 %copy-start = (bf16[2048,512]{1,0:T(8,128)(2,1)S(1)}, bf16[2048,512]{1,0:T(8,128)(2,1)}, u32[]{:S(2)}) copy-start(bf16[2048,512]{1,0:T(8,128)(2,1)} %param.15) | copy-start | bytes 6291460
  9.4 19.9 %all-to-all-start = ((s32[32,32,1]{1,2,0:T(1,128)}), s32[32,32,1]{1,2,0:T(1,128)S(1)}, u32[]{:S(2)}, u32[]{:S(2)}) async-start(s32[32,32,1]{1,2,0:T(1,128)} %all_to_all.41), calls=%async_computation | async-start | bytes 32768 | tf_op jit(solution)/shard_map/all_to_all | solution.py:98
  29.3 33.2 %all-to-all-start.1 = ((bf16[32,32,512]{2,1,0:T(8,128)(2,1)}), bf16[32,32,512]{2,1,0:T(8,128)(2,1)S(1)}, u32[]{:S(2)}, u32[]{:S(2)}) async-start(bf16[32,32,512]{2,1,0:T(8,128)(2,1)} %bitcast.12), calls=%async_computation.1 | async-start | bytes 2097152 | tf_op jit(solution)/shard_map/all_to_all | solution.py:97
  62.5 4.3 %copy-start.2 = (bf16[32,32,512]{2,1,0:T(8,128)(2,1)}, bf16[32,32,512]{2,1,0:T(8,128)(2,1)S(1)}, u32[]{:S(2)}) copy-start(bf16[32,32,512]{2,1,0:T(8,128)(2,1)S(1)} %all-to-all-done.1) | copy-start | bytes 3145732
  62.5 41.0 %all-to-all-start.3 = ((bf16[8,16,8]{1,0,2:T(8,128)(2,1)}), bf16[8,16,8]{1,0,2:T(8,128)(2,1)S(1)}, u32[]{:S(2)}, u32[]{:S(2)}) async-start(bf16[8,16,8]{1,0,2:T(8,128)(2,1)} %compare_convert_fusion), calls=%async_computation.3 | async-start | bytes 32768 | tf_op jit(solution)/shard_map/all_to_all | solution.py:117
  90.8 1.9 copy-start.6
  93.6 1.0 copy-start.3
  103.5 20.7 %all-to-all-start.2 = ((bf16[8,16,8,512]{3,1,0,2:T(8,128)(2,1)}), bf16[8,16,8,512]{3,1,0,2:T(8,128)(2,1)S(1)}, u32[]{:S(2)}, u32[]{:S(2)}) async-start(bf16[8,16,8,512]{3,1,0,2:T(8,128)(2,1)} %copy.123), calls=%async_computation.2 | async-start | bytes 2097152 | tf_op jit(solution)/shard_map/all_to_all | solution.py:110
  125.5 1.4 copy-start.5
  142.9 1.9 copy-start.4
  150.8 19.4 %all-to-all-start.4 = ((bf16[8,8,16,1,512]{4,2,1,3,0:T(8,128)(2,1)}), bf16[8,8,16,1,512]{4,2,1,3,0:T(8,128)(2,1)S(1)}, u32[]{:S(2)}, u32[]{:S(2)}) async-start(bf16[8,8,16,1,512]{4,2,1,3,0:T(8,128)(2,1)} %fusion.64), calls=%async_computation.4 | async-start | bytes 2097152 | tf_op jit(solution)/shard_map/all_to_all | solution.py:126
  176.0 33.4 %all-to-all-start.5 = ((bf16[32,32,512]{2,1,0:T(8,128)(2,1)}), bf16[32,32,512]{2,1,0:T(8,128)(2,1)S(1)}, u32[]{:S(2)}, u32[]{:S(2)}) async-start(bf16[32,32,512]{2,1,0:T(8,128)(2,1)} %broadcast_select_fusion), calls=%async_computation.5 | async-start | bytes 2097152 | tf_op jit(solution)/shard_map/all_to_all | solution.py:130
  181.2 32.8 %copy-start.1 = (bf16[2048,512]{1,0:T(8,128)(2,1)S(1)}, bf16[2048,512]{1,0:T(8,128)(2,1)}, u32[]{:S(2)}) copy-start(bf16[2048,512]{1,0:T(8,128)(2,1)} %param.15) | copy-start | bytes 6291460
